TPU v7x, 32 devices: a whole 2x2x4 slice. The times are simulated.
32 devices in a mesh: dp: 16 (over z, x, core), group: 2 (over y).
Axes of the slice: x: 2, y: 2, z: 4, core: 2. Of those that a mesh axis runs over, the one named last changes fastest.
Arguments:
- inputs: bfloat16 [32768, 2048], P('dp', 'group'), may hold values from -6 to 6
- grad_out: bfloat16 [32768, 2048], P(('dp', 'group')), may hold values from -0.0625 to 0.0625
- weight: bfloat16 [2048, 2048], P('group'), may hold values from -6 to 6
- old_basis: float32 [2048, 256], P('group'), may hold values from -0.125 to 0.125
- first_moment: float32 [256, 2048], P(None, 'dp'), may hold values from -6 to 6
- second_moment: float32 [256, 2048], P(None, 'dp'), may hold values from 0.1 to 3
Outputs:
- new_weight: bfloat16 [2048, 2048], P('group')
- new_first: float32 [256, 2048], P(None, 'dp')
- new_second: float32 [256, 2048], P(None, 'dp')
- new_basis: float32 [2048, 256], P('group')
All inputs are finite; a program needn't handle non-finite values.
Results may differ from a plain program's by a relative error of at most 0.011.
Values may be sent and summed in bfloat16 or wider, within the bound.
No kernel may reach another device: no remote copies, remote signals or barrier semaphores. Data moves between devices by JAX's collectives and lax.ppermute only.
A program may use at most 64 MiB of HBM per device.

v0:
```python
import jax
import jax.numpy as jnp
from jax import lax
from jax.sharding import PartitionSpec as P

NS_STEPS = 5
STEP = 10
BETA_ONE = 0.9
BETA_TWO = 0.99
ADAM_EPS = 1e-08
HIGHEST = lax.Precision.HIGHEST


def matmul(left, right):
    return jnp.dot(left, right, precision=HIGHEST)


def inner_gram(matrix):
    return lax.dot_general(matrix, matrix, (((0,), (0,)), ((), ())), precision=HIGHEST)


def refine_group(subspace):
    squares = lax.psum(jnp.sum(subspace * subspace), "group")
    iterate = subspace / jnp.sqrt(squares)
    for sweep in range(NS_STEPS):
        gram = lax.psum(inner_gram(iterate).astype(jnp.bfloat16), "group").astype(jnp.float32)
        iterate = 1.5 * iterate - 0.5 * matmul(iterate, gram)
    return iterate


def shards(inputs, grad_out, weight, old_basis, first_moment, second_moment):
    partial_grad = lax.dot_general(
        inputs,
        lax.all_gather(grad_out, "group", axis=0, tiled=True),
        (((0,), (0,)), ((), ())),
        preferred_element_type=jnp.float32,
    )
    grad_block = lax.psum_scatter(partial_grad, "dp", scatter_dimension=1, tiled=True)
    projected = lax.psum(matmul(old_basis.T, grad_block).astype(jnp.bfloat16), "group").astype(
        jnp.float32
    )
    new_first = BETA_ONE * first_moment + (1.0 - BETA_ONE) * projected
    new_second = BETA_TWO * second_moment + (1.0 - BETA_TWO) * projected * projected
    direction = (
        new_first
        / (1.0 - BETA_ONE**STEP)
        / (jnp.sqrt(new_second / (1.0 - BETA_TWO**STEP)) + ADAM_EPS)
    )
    col_count = grad_block.shape[1]
    col_offset = lax.axis_index("dp") * col_count
    own_cols = lax.dynamic_slice_in_dim(weight, col_offset, col_count, 1).astype(jnp.float32)
    updated = (own_cols - matmul(old_basis, direction)).astype(jnp.bfloat16)
    new_weight = lax.all_gather(updated, "dp", axis=1, tiled=True)
    subspace_terms = matmul(grad_block, projected.T)
    subspace = lax.psum(subspace_terms, "dp")
    new_basis = refine_group(subspace)
    return (new_weight, new_first, new_second, new_basis)


def solution(mesh):
    return jax.shard_map(
        shards,
        mesh=mesh,
        in_specs=(
            P("dp", "group"),
            P(("dp", "group"), None),
            P("group", None),
            P("group", None),
            P(None, "dp"),
            P(None, "dp"),
        ),
        out_specs=(P("group", None), P(None, "dp"), P(None, "dp"), P("group", None)),
        check_vma=False,
    )
```

profile of v0, /device:TPU:0, one launch (start us, length us, event | category | flops | bytes accessed | tf_op | source)
XLA Modules:
  0.0 558.3 jit_solution(406713574473706663)
XLA Ops:
  8.0 108.3 %all-gather.3.cloned.1.call-done = bf16[2048,2048]{1,0:T(8,128)(2,1)} async-done(((bf16[1024,2048]{1,0:T(8,128)(2,1)}), bf16[2048,2048]{1,0:T(8,128)(2,1)}) %all-gather.3.cloned.1.call-update) | async-done | bytes 8388624 | tf_op jit(solution)/shard_map/all_gather | solution.py:34
  116.3 14.6 %fusion.21 = f32[1024,2048]{1,0:T(8,128)} fusion(bf16[2048,1024]{1,0:T(8,128)(2,1)} %param.6, bf16[2048,2048]{1,0:T(8,128)(2,1)} %all-gather.3.cloned.1.call-done), kind=kOutput, calls=%fused_computation.38 | convolution fusion | flops 8589934592 | bytes 20971520 | tf_op jit(solution)/shard_map/dot_general | solution.py:32
  130.9 103.7 %reduce-scatter.2.cloned.1.call-done = f32[1024,128]{1,0:T(8,128)} async-done(((f32[1024,2048]{1,0:T(8,128)}), f32[1024,128]{1,0:T(8,128)}) %reduce-scatter.2.cloned.1.call-update) | async-done | bytes 524304 | tf_op jit(solution)/shard_map/reduce_scatter | solution.py:38
  234.6 2.7 fusion.7
  237.4 20.7 %all-reduce.8.cloned.1.call-done = bf16[256,128]{0,1:T(8,128)(2,1)} async-done(((bf16[256,128]{0,1:T(8,128)(2,1)}), bf16[256,128]{0,1:T(8,128)(2,1)}) %all-reduce.8.cloned.1.call-update) | async-done | bytes 65552 | tf_op jit(solution)/shard_map/psum | solution.py:39
  258.1 2.6 fusion.22
  260.8 95.1 %all-reduce.10.cloned.1.call-done = f32[1024,256]{1,0:T(8,128)} async-done(((f32[1024,256]{1,0:T(8,128)}), f32[1024,256]{1,0:T(8,128)}) %all-reduce.10.cloned.1.call-update) | async-done | bytes 1048592 | tf_op jit(solution)/shard_map/psum | solution.py:55
  355.8 2.2 multiply_reduce_fusion
  358.0 5.5 psum.58
  364.3 4.0 convolution_convert_fusion.4
  368.4 20.7 %all-reduce.12.cloned.1.call-done = bf16[256,256]{1,0:T(8,128)(2,1)} async-done(((bf16[256,256]{1,0:T(8,128)(2,1)}), bf16[256,256]{1,0:T(8,128)(2,1)}) %all-reduce.12.cloned.1.call-update) | async-done | bytes 131088 | tf_op jit(solution)/shard_map/psum | solution.py:26
  389.1 1.6 fusion.4
  390.7 2.5 convolution_convert_fusion.3
  393.5 21.4 %all-reduce.14.cloned.1.call-done = bf16[256,256]{1,0:T(8,128)(2,1)} async-done(((bf16[256,256]{1,0:T(8,128)(2,1)}), bf16[256,256]{1,0:T(8,128)(2,1)}) %all-reduce.14.cloned.1.call-update) | async-done | bytes 131088 | tf_op jit(solution)/shard_map/psum | solution.py:26
  416.4 2.5 convolution_convert_fusion.2
  421.7 18.9 %all-reduce.16.cloned.1.call-done = bf16[256,256]{1,0:T(8,128)(2,1)} async-done(((bf16[256,256]{1,0:T(8,128)(2,1)}), bf16[256,256]{1,0:T(8,128)(2,1)}) %all-reduce.16.cloned.1.call-update) | async-done | bytes 131088 | tf_op jit(solution)/shard_map/psum | solution.py:26
  442.2 2.5 convolution_convert_fusion.1
  445.7 20.6 %all-reduce.18.cloned.1.call-done = bf16[256,256]{1,0:T(8,128)(2,1)} async-done(((bf16[256,256]{1,0:T(8,128)(2,1)}), bf16[256,256]{1,0:T(8,128)(2,1)}) %all-reduce.18.cloned.1.call-update) | async-done | bytes 131088 | tf_op jit(solution)/shard_map/psum | solution.py:26
  467.9 2.5 convolution_convert_fusion
  470.5 2.9 fusion.6
  474.9 17.2 %all-reduce.20.cloned.1.call-done = bf16[256,256]{1,0:T(8,128)(2,1)} async-done(((bf16[256,256]{1,0:T(8,128)(2,1)}), bf16[256,256]{1,0:T(8,128)(2,1)}) %all-reduce.20.cloned.1.call-update) | async-done | bytes 131088 | tf_op jit(solution)/shard_map/psum | solution.py:26
  492.1 2.5 fusion
  494.6 50.5 %all-gather.5.cloned.1.call-done = bf16[1024,2048]{0,1:T(8,128)(2,1)} async-done(((bf16[1024,128]{0,1:T(8,128)(2,1)}), bf16[1024,2048]{0,1:T(8,128)(2,1)}) %all-gather.5.cloned.1.call-update) | async-done | bytes 4194320 | tf_op jit(solution)/shard_map/all_gather | solution.py:53
  545.1 6.4 %copy.13 = bf16[1024,2048]{1,0:T(8,128)(2,1)} copy(bf16[1024,2048]{0,1:T(8,128)(2,1)} %all-gather.5.cloned.1.call-done) | data formatting | bytes 8388608
  (38 shorter events, 11.2 us)
Async XLA Ops:
  7.2 227.5 %copy-start = (f32[1024,256]{1,0:T(8,128)S(1)}, f32[1024,256]{1,0:T(8,128)}, u32[]{:S(2)}) copy-start(f32[1024,256]{1,0:T(8,128)} %param.9) | copy-start | bytes 3145732
  7.2 109.1 %all-gather.3.cloned.1.call-start = ((), (), s32[]{:S(2)}) async-start(), calls=%async_computation.1 | async-start | bytes 12582912 | tf_op jit(solution)/shard_map/all_gather | solution.py:34
  7.9 226.7 %reduce-scatter.2.cloned.1.call-start = ((), (), s32[]{:S(2)}) async-start(), calls=%async_computation.2 | async-start | bytes 8912896 | tf_op jit(solution)/shard_map/reduce_scatter | solution.py:38
  130.9 127.2 %all-reduce.8.cloned.1.call-start = ((), (), s32[]{:S(2)}) async-start(), calls=%async_computation.3 | async-start | bytes 131072 | tf_op jit(solution)/shard_map/psum | solution.py:39
  237.4 118.5 %all-reduce.10.cloned.1.call-start = ((), (), s32[]{:S(2)}) async-start(), calls=%async_computation.5 | async-start | bytes 2097152 | tf_op jit(solution)/shard_map/psum | solution.py:55
  260.7 128.4 %all-reduce.12.cloned.1.call-start = ((), (), s32[]{:S(2)}) async-start(), calls=%async_computation.6 | async-start | bytes 262144 | tf_op jit(solution)/shard_map/psum | solution.py:26
  355.8 33.3 %copy-start.1 = (f32[1024,256]{1,0:T(8,128)S(1)}, f32[1024,256]{1,0:T(8,128)}, u32[]{:S(2)}) copy-start(f32[1024,256]{1,0:T(8,128)} %all-reduce.10.cloned.1.call-done) | copy-start | bytes 3145732
  368.3 46.6 %all-reduce.14.cloned.1.call-start = ((), (), s32[]{:S(2)}) async-start(), calls=%async_computation.7 | async-start | bytes 262144 | tf_op jit(solution)/shard_map/psum | solution.py:26
  390.7 30.2 %copy-start.2 = (f32[256,128]{1,0:T(8,128)S(1)}, f32[256,128]{1,0:T(8,128)}, u32[]{:S(2)}) copy-start(f32[256,128]{1,0:T(8,128)} %param.10) | copy-start | bytes 393220
  390.7 30.3 %copy-start.3 = (f32[256,128]{1,0:T(8,128)S(1)}, f32[256,128]{1,0:T(8,128)}, u32[]{:S(2)}) copy-start(f32[256,128]{1,0:T(8,128)} %param.11) | copy-start | bytes 393220
  393.2 47.4 %all-reduce.16.cloned.1.call-start = ((), (), s32[]{:S(2)}) async-start(), calls=%async_computation.8 | async-start | bytes 262144 | tf_op jit(solution)/shard_map/psum | solution.py:26
  419.0 47.4 %all-reduce.18.cloned.1.call-start = ((), (), s32[]{:S(2)}) async-start(), calls=%async_computation.9 | async-start | bytes 262144 | tf_op jit(solution)/shard_map/psum | solution.py:26
  444.7 47.4 %all-reduce.20.cloned.1.call-start = ((), (), s32[]{:S(2)}) async-start(), calls=%async_computation.10 | async-start | bytes 262144 | tf_op jit(solution)/shard_map/psum | solution.py:26
  470.4 74.7 %all-gather.5.cloned.1.call-start = ((), (), s32[]{:S(2)}) async-start(), calls=%async_computation.4 | async-start | bytes 4456448 | tf_op jit(solution)/shard_map/all_gather | solution.py:53
Sparse Core Ops, SparseCore 0:
  9.5 106.6 all-gather.2
  131.0 103.5 reduce-scatter.1
  237.5 20.5 all-reduce.7
  262.0 93.7 all-reduce.9
  368.4 20.6 all-reduce.11
  393.4 21.5 all-reduce.13
  419.1 21.5 all-reduce.15
  444.8 21.5 all-reduce.17
  470.5 21.5 all-reduce.19
  494.7 50.3 all-gather.4
where the time goes:
time: 559 us; the launch traced here: 558 us
  waiting for transfers between devices  478 us (86%)
  matrix products  45.4 us (8%)
  between operations  15 us (3%)
  local copies, waits for them, and re-layouts  10.6 us (2%)
    all_gather x1, waiting for transfers between devices, shards(): lax.all_gather(grad_out, 'group', axis=0, tiled=True)  108 us
    reduce_scatter x1, waiting for transfers between devices, shards(): lax.psum_scatter(partial_grad, 'dp', scatter_dimension=1, tiled=True)  104 us
    psum x5, waiting for transfers between devices, refine_group(): lax.psum(inner_gram(iterate).astype(jnp.bfloat16), 'group')  99 us
    psum x1, waiting for transfers between devices, shards(): subspace = lax.psum(subspace_terms, 'dp')  95.1 us
    all_gather x1, waiting for transfers between devices, shards(): new_weight = lax.all_gather(updated, 'dp', axis=1, tiled=True)  50.5 us
    psum x1, waiting for transfers between devices, shards(): lax.psum(matmul(old_basis.T, grad_block).astype(jnp.bfloat16), 'group')  20.7 us
    dot_general x8, matrix products, matmul(): return jnp.dot(left, right, precision=HIGHEST)  16.8 us
    dot_general x1, matrix products, shards(): lax.dot_general(inputs, lax.all_gather(grad_out, 'group', axis=0, tiled=T...  14.6 us
  transfers between devices with their start and end apart: 10, of which 10 were waited for; matrix products, arithmetic and copies ran while one was open for 2% of the time, Pallas kernels for 0%

commit v1 on v0

--- a/solution.py
+++ b/solution.py
@@ -36,9 +36,9 @@
         preferred_element_type=jnp.float32,
     )
     grad_block = lax.psum_scatter(partial_grad, "dp", scatter_dimension=1, tiled=True)
-    projected = lax.psum(matmul(old_basis.T, grad_block).astype(jnp.bfloat16), "group").astype(
-        jnp.float32
-    )
+    projected = jnp.sum(
+        lax.all_gather(matmul(old_basis.T, grad_block).astype(jnp.bfloat16), "group"), axis=0
+    ).astype(jnp.float32)
     new_first = BETA_ONE * first_moment + (1.0 - BETA_ONE) * projected
     new_second = BETA_TWO * second_moment + (1.0 - BETA_TWO) * projected * projected
     direction = (

time: 559 us -> 541 us (0.968)
  waiting for transfers between devices: 478 us -> 455 us
    psum x1 -> x0, waiting for transfers between devices: 20.7 us -> none  [shards(): lax.psum(matmul(old_basis.T, grad_block).astype(jnp.bfloat16), 'group')]
  transfers between devices with their start and end apart: 10 -> 9, of which waited for: 10 -> 9; matrix products, arithmetic and copies ran while one was open for 2% -> 2% of each run, Pallas kernels for 0% -> 0%
where the time goes in v1:
time: 541 us
  waiting for transfers between devices  455 us (84%)
  matrix products  44.9 us (8%)
  between operations  14.6 us (3%)
  local copies, waits for them, and re-layouts  11.3 us (2%)
  blocking collectives  10.5 us (2%)
    all_gather x1, waiting for transfers between devices, shards(): lax.all_gather(grad_out, 'group', axis=0, tiled=True)  108 us
    reduce_scatter x1, waiting for transfers between devices, shards(): lax.psum_scatter(partial_grad, 'dp', scatter_dimension=1, tiled=True)  104 us
    psum x5, waiting for transfers between devices, refine_group(): lax.psum(inner_gram(iterate).astype(jnp.bfloat16), 'group')  98.3 us
    psum x1, waiting for transfers between devices, shards(): subspace = lax.psum(subspace_terms, 'dp')  93.4 us
    all_gather x1, waiting for transfers between devices, shards(): new_weight = lax.all_gather(updated, 'dp', axis=1, tiled=True)  50.6 us
    dot_general x8, matrix products, matmul(): return jnp.dot(left, right, precision=HIGHEST)  16.2 us
    dot_general x1, matrix products, shards(): lax.dot_general(inputs, lax.all_gather(grad_out, 'group', axis=0, tiled=T...  14.7 us
    dot_general x5, matrix products, inner_gram(): lax.dot_general(matrix, matrix, (((0,), (0,)), ((), ())), precision=HIGHEST)  14 us
  transfers between devices with their start and end apart: 9, of which 9 were waited for; matrix products, arithmetic and copies ran while one was open for 2% of the time, Pallas kernels for 0%

profile of v1, /device:TPU:0, one launch (start us, length us, event | category | flops | bytes accessed | tf_op | source)
XLA Modules:
  0.0 540.6 jit_solution(15344716914715569727)
XLA Ops:
  8.0 108.3 %all-gather.4.cloned.1.call-done = bf16[2048,2048]{1,0:T(8,128)(2,1)} async-done(((bf16[1024,2048]{1,0:T(8,128)(2,1)}), bf16[2048,2048]{1,0:T(8,128)(2,1)}) %all-gather.4.cloned.1.call-update) | async-done | bytes 8388624 | tf_op jit(solution)/shard_map/all_gather | solution.py:34
  116.3 14.7 %fusion.21 = f32[1024,2048]{1,0:T(8,128)} fusion(bf16[2048,1024]{1,0:T(8,128)(2,1)} %param.6, bf16[2048,2048]{1,0:T(8,128)(2,1)} %all-gather.4.cloned.1.call-done), kind=kOutput, calls=%fused_computation.38 | convolution fusion | flops 8589934592 | bytes 20971520 | tf_op jit(solution)/shard_map/dot_general | solution.py:32
  131.1 103.7 %reduce-scatter.2.cloned.1.call-done = f32[1024,128]{1,0:T(8,128)} async-done(((f32[1024,2048]{1,0:T(8,128)}), f32[1024,128]{1,0:T(8,128)}) %reduce-scatter.2.cloned.1.call-update) | async-done | bytes 524304 | tf_op jit(solution)/shard_map/reduce_scatter | solution.py:38
  234.8 2.1 fusion.7
  236.8 4.9 all-gather
  242.1 2.6 fusion.22
  244.8 93.4 %all-reduce.7.cloned.1.call-done = f32[1024,256]{1,0:T(8,128)} async-done(((f32[1024,256]{1,0:T(8,128)}), f32[1024,256]{1,0:T(8,128)}) %all-reduce.7.cloned.1.call-update) | async-done | bytes 1048592 | tf_op jit(solution)/shard_map/psum | solution.py:55
  338.2 2.2 multiply_reduce_fusion
  340.4 5.5 %psum.50 = f32[]{:T(128)} all-reduce(f32[]{:T(128)} %multiply_reduce_fusion), channel_id=1, replica_groups=mesh['dp'=16,'group'=2] {'group'}, use_global_device_ids=true, to_apply=%region_4.0 | all-reduce | flops 1 | bytes 8 | tf_op jit(solution)/shard_map/psum | solution.py:23
  346.6 4.0 convolution_convert_fusion.4
  350.8 20.7 %all-reduce.9.cloned.1.call-done = bf16[256,256]{1,0:T(8,128)(2,1)} async-done(((bf16[256,256]{1,0:T(8,128)(2,1)}), bf16[256,256]{1,0:T(8,128)(2,1)}) %all-reduce.9.cloned.1.call-update) | async-done | bytes 131088 | tf_op jit(solution)/shard_map/psum | solution.py:26
  371.5 1.6 fusion.4
  373.1 2.5 convolution_convert_fusion.3
  375.8 21.4 %all-reduce.11.cloned.1.call-done = bf16[256,256]{1,0:T(8,128)(2,1)} async-done(((bf16[256,256]{1,0:T(8,128)(2,1)}), bf16[256,256]{1,0:T(8,128)(2,1)}) %all-reduce.11.cloned.1.call-update) | async-done | bytes 131088 | tf_op jit(solution)/shard_map/psum | solution.py:26
  398.8 2.5 convolution_convert_fusion.2
  404.7 18.3 %all-reduce.13.cloned.1.call-done = bf16[256,256]{1,0:T(8,128)(2,1)} async-done(((bf16[256,256]{1,0:T(8,128)(2,1)}), bf16[256,256]{1,0:T(8,128)(2,1)}) %all-reduce.13.cloned.1.call-update) | async-done | bytes 131088 | tf_op jit(solution)/shard_map/psum | solution.py:26
  424.5 2.5 convolution_convert_fusion.1
  428.1 20.6 %all-reduce.15.cloned.1.call-done = bf16[256,256]{1,0:T(8,128)(2,1)} async-done(((bf16[256,256]{1,0:T(8,128)(2,1)}), bf16[256,256]{1,0:T(8,128)(2,1)}) %all-reduce.15.cloned.1.call-update) | async-done | bytes 131088 | tf_op jit(solution)/shard_map/psum | solution.py:26
  450.3 2.5 convolution_convert_fusion
  452.8 2.9 fusion.6
  457.3 17.2 %all-reduce.17.cloned.1.call-done = bf16[256,256]{1,0:T(8,128)(2,1)} async-done(((bf16[256,256]{1,0:T(8,128)(2,1)}), bf16[256,256]{1,0:T(8,128)(2,1)}) %all-reduce.17.cloned.1.call-update) | async-done | bytes 131088 | tf_op jit(solution)/shard_map/psum | solution.py:26
  474.5 2.5 fusion
  477.0 50.6 %all-gather.6.cloned.1.call-done = bf16[1024,2048]{0,1:T(8,128)(2,1)} async-done(((bf16[1024,128]{0,1:T(8,128)(2,1)}), bf16[1024,2048]{0,1:T(8,128)(2,1)}) %all-gather.6.cloned.1.call-update) | async-done | bytes 4194320 | tf_op jit(solution)/shard_map/all_gather | solution.py:53
  527.6 6.4 %copy.15 = bf16[1024,2048]{1,0:T(8,128)(2,1)} copy(bf16[1024,2048]{0,1:T(8,128)(2,1)} %all-gather.6.cloned.1.call-done) | data formatting | bytes 8388608
  (38 shorter events, 12.2 us)
Async XLA Ops:
  7.2 227.6 %copy-start = (f32[1024,256]{1,0:T(8,128)S(1)}, f32[1024,256]{1,0:T(8,128)}, u32[]{:S(2)}) copy-start(f32[1024,256]{1,0:T(8,128)} %param.9) | copy-start | bytes 3145732
  7.2 109.1 %all-gather.4.cloned.1.call-start = ((), (), s32[]{:S(2)}) async-start(), calls=%async_computation.1 | async-start | bytes 12582912 | tf_op jit(solution)/shard_map/all_gather | solution.py:34
  7.9 226.8 %reduce-scatter.2.cloned.1.call-start = ((), (), s32[]{:S(2)}) async-start(), calls=%async_computation.2 | async-start | bytes 8912896 | tf_op jit(solution)/shard_map/reduce_scatter | solution.py:38
  131.0 207.2 %all-reduce.7.cloned.1.call-start = ((), (), s32[]{:S(2)}) async-start(), calls=%async_computation.4 | async-start | bytes 2097152 | tf_op jit(solution)/shard_map/psum | solution.py:55
  244.8 126.7 %all-reduce.9.cloned.1.call-start = ((), (), s32[]{:S(2)}) async-start(), calls=%async_computation.5 | async-start | bytes 262144 | tf_op jit(solution)/shard_map/psum | solution.py:26
  338.2 33.3 %copy-start.1 = (f32[1024,256]{1,0:T(8,128)S(1)}, f32[1024,256]{1,0:T(8,128)}, u32[]{:S(2)}) copy-start(f32[1024,256]{1,0:T(8,128)} %all-reduce.7.cloned.1.call-done) | copy-start | bytes 3145732
  350.7 46.6 %all-reduce.11.cloned.1.call-start = ((), (), s32[]{:S(2)}) async-start(), calls=%async_computation.6 | async-start | bytes 262144 | tf_op jit(solution)/shard_map/psum | solution.py:26
  373.1 30.2 %copy-start.2 = (f32[256,128]{1,0:T(8,128)S(1)}, f32[256,128]{1,0:T(8,128)}, u32[]{:S(2)}) copy-start(f32[256,128]{1,0:T(8,128)} %param.10) | copy-start | bytes 393220
  373.1 30.9 %copy-start.3 = (f32[256,128]{1,0:T(8,128)S(1)}, f32[256,128]{1,0:T(8,128)}, u32[]{:S(2)}) copy-start(f32[256,128]{1,0:T(8,128)} %param.11) | copy-start | bytes 393220
  375.6 47.4 %all-reduce.13.cloned.1.call-start = ((), (), s32[]{:S(2)}) async-start(), calls=%async_computation.7 | async-start | bytes 262144 | tf_op jit(solution)/shard_map/psum | solution.py:26
  401.3 47.4 %all-reduce.15.cloned.1.call-start = ((), (), s32[]{:S(2)}) async-start(), calls=%async_computation.8 | async-start | bytes 262144 | tf_op jit(solution)/shard_map/psum | solution.py:26
  427.1 47.4 %all-reduce.17.cloned.1.call-start = ((), (), s32[]{:S(2)}) async-start(), calls=%async_computation.9 | async-start | bytes 262144 | tf_op jit(solution)/shard_map/psum | solution.py:26
  452.8 74.8 %all-gather.6.cloned.1.call-start = ((), (), s32[]{:S(2)}) async-start(), calls=%async_computation.3 | async-start | bytes 4456448 | tf_op jit(solution)/shard_map/all_gather | solution.py:53
Sparse Core Ops, SparseCore 0:
  9.5 106.6 all-gather.3
  131.1 103.5 reduce-scatter.1
  244.9 93.2 all-reduce.6
  350.8 20.6 all-reduce.8
  375.7 21.5 all-reduce.10
  401.5 21.5 all-reduce.12
  427.2 21.5 all-reduce.14
  452.9 21.5 all-reduce.16
  477.2 50.3 all-gather.5
